TPU v7x, 32 devices: a whole 2x2x4 slice. The times are simulated.
32 devices in a mesh: group: 2 (over y), seq: 4 (over z), batch: 2 (over x), chan: 2 (over core).
Axes of the slice: x: 2, y: 2, z: 4, core: 2. Of those that a mesh axis runs over, the one named last changes fastest.
Arguments:
- seq_in: bfloat16 [4, 4096, 768], P(('group', 'batch'), 'seq', 'chan'), parts along dimension 0, may hold values from -6 to 6
- conv_weight: bfloat16 [3, 768, 768], P(None, 'chan'), may hold values from -0.125 to 0.125
- cotangent: bfloat16 [4, 2048, 768], P(('group', 'batch'), 'seq', 'chan'), parts along dimension 0, may hold values from -0.59765625 to 0.59765625
Outputs:
- block_out: bfloat16 [4, 2048, 768], P(('group', 'batch'), 'seq', 'chan'), parts along dimension 0
- input_grad: bfloat16 [4, 4096, 768], P(('group', 'batch'), 'seq', 'chan'), parts along dimension 0
- weight_grad: float32 [6, 768, 768], P('group', 'chan', 'batch'), parts along dimension 0
There are 2 independent parts, one for each index of `group`. A program takes and returns all parts, laid end to end along the dimension named above; an argument that names none is the same for every part. Nothing has to cross between parts.
All inputs are finite; a program needn't handle non-finite values.
Results may differ from a plain program's by a relative error of at most 0.0031.
Values may be sent and summed in bfloat16 or wider, within the bound.
No kernel may reach another device: no remote copies, remote signals or barrier semaphores. Data moves between devices by JAX's collectives and lax.ppermute only.
A program may use at most 64 MiB of HBM per device.

v0:
```python
import jax
import jax.numpy as jnp
from jax import lax
from jax.sharding import PartitionSpec as P


def shift_from(block, axis, distance):
    size = lax.axis_size(axis)
    route = [(i - distance, i) for i in range(size) if 0 <= i - distance < size]
    return lax.ppermute(block, axis, route)


def half_of(array, index, axis):
    parts = 2
    shape = array.shape
    split = shape[:axis] + (parts, shape[axis] // parts) + shape[axis + 1 :]
    return lax.dynamic_index_in_dim(array.reshape(split), index, axis, keepdims=False)


def shards(seq_in, conv_weight, cotangent):
    local_in = seq_in[0]
    local_cot = cotangent[0]
    rows = local_in.shape[0] // 2
    width = local_in.shape[1]
    spread = rows // 2
    pooled = 0.5 * jnp.sum(local_in.astype(jnp.float32).reshape(rows, 2, width), axis=1)
    activation = jax.nn.gelu(pooled).astype(jnp.bfloat16)
    both = jnp.stack([activation, local_cot])
    from_prev = shift_from(both[:, rows - spread :], "seq", 1)
    from_next = shift_from(both[:, :spread], "seq", -1)
    own_ext = jnp.concatenate([from_prev, both, from_next], 1)
    full_ext = lax.all_gather(own_ext, "chan", axis=2, tiled=True)
    act_full, cot_full = (full_ext[0], full_ext[1])
    weight_cols = lax.all_to_all(conv_weight, "chan", 2, 1, tiled=True)
    act_taps = jnp.stack([act_full[k * spread : k * spread + rows] for k in range(3)], 1)
    conv_out = jnp.dot(
        act_taps.reshape(rows, -1),
        weight_cols.reshape(-1, weight_cols.shape[2]),
        preferred_element_type=jnp.float32,
    )
    block_out = (pooled + conv_out).astype(jnp.bfloat16)
    cot_taps = jnp.stack(
        [cot_full[(2 - k) * spread : (2 - k) * spread + rows] for k in range(3)], 1
    )
    activ_grad = jnp.einsum(
        "tko,kio->ti", cot_taps, conv_weight, preferred_element_type=jnp.float32
    )
    unused, gelu_back = jax.vjp(jax.nn.gelu, pooled)
    pooled_grad = local_cot.astype(jnp.float32) + gelu_back(activ_grad)[0]
    input_grad = jnp.repeat(0.5 * pooled_grad, 2, axis=0).astype(jnp.bfloat16)
    own_taps = jnp.stack([own_ext[0, k * spread : k * spread + rows] for k in range(3)], 1)
    cot_mid = cot_full[spread : spread + rows]
    batch_count = lax.axis_size("batch")
    if batch_count == 2:
        b = lax.axis_index("batch")
        send = jnp.einsum(
            "tki,to->kio", own_taps, half_of(cot_mid, 1 - b, 1), preferred_element_type=jnp.float32
        )
        keep = jnp.einsum(
            "tki,to->kio", own_taps, half_of(cot_mid, b, 1), preferred_element_type=jnp.float32
        )
        summed = keep + lax.ppermute(send, "batch", [(0, 1), (1, 0)])
    else:
        partial = jnp.einsum("tki,to->kio", own_taps, cot_mid, preferred_element_type=jnp.float32)
        summed = lax.psum_scatter(partial, "batch", scatter_dimension=2, tiled=True)
    weight_grad = lax.psum(summed, "seq")
    return (block_out[None], input_grad[None], weight_grad)


def solution(mesh):
    in_specs = (
        P(("group", "batch"), "seq", "chan"),
        P(None, "chan", None),
        P(("group", "batch"), "seq", "chan"),
    )
    out_specs = (
        P(("group", "batch"), "seq", "chan"),
        P(("group", "batch"), "seq", "chan"),
        P("group", "chan", "batch"),
    )
    return jax.shard_map(shards, mesh=mesh, in_specs=in_specs, out_specs=out_specs, check_vma=False)
```

profile of v0, /device:TPU:0, one launch (start us, length us, event | category | flops | bytes accessed | tf_op | source)
XLA Modules:
  0.0 179.5 jit_solution(5351627847527597983)
XLA Ops:
  7.2 2.2 %reshape.129 = f32[512,2,384]{2,1,0:T(2,128)S(1)} reshape(bf16[1,1024,384]{2,1,0:T(8,128)(2,1)} %param.3) | data formatting | bytes 2359296 | tf_op jit(solution)/shard_map/convert_element_type | solution.py:26
  9.4 1.9 %reduce_sum.9 = f32[512,384]{1,0:T(8,128)S(1)} reduce(f32[512,2,384]{2,1,0:T(2,128)S(1)} %reshape.129, f32[]{:T(128)} %constant.8.clone.1), dimensions={1}, to_apply=%region_0.0 | reduce | flops 196608 | bytes 2359300 | tf_op jit(solution)/shard_map/reduce_sum | solution.py:26
  11.7 5.0 %collective-permute-start = (bf16[2,256,384]{2,1,0:T(8,128)(2,1)S(1)}, bf16[2,256,384]{2,1,0:T(8,128)(2,1)S(1)}, u32[]{:S(2)}, u32[]{:S(2)}) collective-permute-start(bf16[2,256,384]{2,1,0:T(8,128)(2,1)S(1)} %get-tuple-element.14), channel_id=1, source_target_pairs={{0,4},{4,8},{8,12},{1,5},{5,9},{9,13},{2,6},{6,10},{10,14},{3,7},{... | collective-permute-start | bytes 1179656 | tf_op jit(solution)/shard_map/ppermute | solution.py:10
  16.7 1.3 collective-permute-start.1
  18.0 7.0 %collective-permute-done = bf16[2,256,384]{2,1,0:T(8,128)(2,1)S(1)} collective-permute-done((bf16[2,256,384]{2,1,0:T(8,128)(2,1)S(1)}, bf16[2,256,384]{2,1,0:T(8,128)(2,1)S(1)}, u32[]{:S(2)}, u32[]{:S(2)}) %collective-permute-start) | collective-permute-done | bytes 393248 | tf_op jit(solution)/shard_map/ppermute | solution.py:10
  25.0 4.1 %collective-permute-done.1 = bf16[2,256,384]{2,1,0:T(8,128)(2,1)S(1)} collective-permute-done((bf16[2,256,384]{2,1,0:T(8,128)(2,1)S(1)}, bf16[2,256,384]{2,1,0:T(8,128)(2,1)S(1)}, u32[]{:S(2)}, u32[]{:S(2)}) %collective-permute-start.1) | collective-permute-done | bytes 393248 | tf_op jit(solution)/shard_map/ppermute | solution.py:10
  29.1 1.3 pad_maximum_fusion.1
  30.5 1.0 fusion.35
  31.6 11.2 %all-gather.2.cloned.1.call-done = bf16[2,1024,768]{2,1,0:T(8,128)(2,1)} async-done(((bf16[2,1024,384]{2,1,0:T(8,128)(2,1)}), bf16[2,1024,768]{2,1,0:T(8,128)(2,1)}) %all-gather.2.cloned.1.call-update) | async-done | bytes 3145744 | tf_op jit(solution)/shard_map/all_gather | solution.py:32
  42.8 4.6 %fusion.45 = (bf16[1,512,768]{2,1,0:T(8,128)(2,1)S(1)}, bf16[512,1,768]{2,0,1:T(8,128)(2,1)}, bf16[512,1,768]{2,0,1:T(8,128)(2,1)}, bf16[512,1,768]{2,0,1:T(8,12...) fusion(bf16[2,1024,768]{2,1,0:T(8,128)(2,1)} %all-gather.2.cloned.1.call-done), kind=kLoop, calls=%fused_computation.67 | loop fusion | bytes 10223616 | tf_op jit(solution)/shard_map/slice | solution.py:43
  47.6 1.6 constant_dynamic-slice_fusion.1
  50.1 1.8 %collective-permute-start.2 = (f32[3,384,384]{2,1,0:T(8,128)S(1)}, f32[3,384,384]{2,1,0:T(8,128)S(1)}, u32[]{:S(2)}, u32[]{:S(2)}) collective-permute-start(f32[3,384,384]{2,1,0:T(8,128)S(1)} %fusion.38), channel_id=1, source_target_pairs={{0,2},{2,0},{1,3},{3,1},{4,6},{6,4},{5,7},{7,5},{8,10},{10,8},{9,1... | collective-permute-start | bytes 5308424 | tf_op jit(solution)/shard_map/ppermute | solution.py:62
  51.9 39.1 %collective-permute-done.2 = f32[3,384,384]{2,1,0:T(8,128)S(1)} collective-permute-done((f32[3,384,384]{2,1,0:T(8,128)S(1)}, f32[3,384,384]{2,1,0:T(8,128)S(1)}, u32[]{:S(2)}, u32[]{:S(2)}) %collective-permute-start.2) | collective-permute-done | bytes 1769504 | tf_op jit(solution)/shard_map/ppermute | solution.py:62
  91.0 2.0 %convolution_add_fusion = f32[3,384,384]{2,1,0:T(8,128)} fusion(f32[3,384,384]{2,1,0:T(8,128)S(1)} %collective-permute-done.2, bf16[512,1,384]{2,0,1:T(8,128)(2,1)S(1)} %get-tuple-element.13, bf16[512,1,384]{2,0,1:T(8,128)(2,1)S(1)} %copy-done.1, bf16[512,1,384]{2,0,1:T(8,128)(2,1)S(1)} %get-tuple-element.12, bf16[512,1,384]{2,1,0:T(2,128)(2,1)S(1)} %get-tuple-element.10), kind=kOutput, calls=%fused_computation.8 | convolution fusion | flops 454606848 | bytes 5111808 | tf_op jit(solution)/shard_map/tki,to->kio/dot_general | solution.py:59
  93.0 4.0 %copy.21 = bf16[3,384,768]{1,0,2:T(4,128)(2,1)S(1)} copy(bf16[3,384,768]{2,1,0:T(8,128)(2,1)} %param.4) | data formatting | bytes 3538944 | tf_op args[1]
  97.0 5.6 %all_to_all.15 = bf16[3,384,768]{1,0,2:T(4,128)(2,1)S(1)} all-to-all(bf16[3,384,768]{1,0,2:T(4,128)(2,1)S(1)} %copy.21), channel_id=1, replica_groups=mesh['group'=2,'seq'=4,'batch'=2,'chan'=2] {'chan'}, dimensions={2} | all-to-all | bytes 3538944 | tf_op jit(solution)/shard_map/all_to_all | solution.py:34
  102.9 2.3 %copy.23 = bf16[3,2,384,384]{3,2,1,0:T(8,128)(2,1)} copy(bf16[3,2,384,384]{2,3,1,0:T(8,128)(2,1)S(1)} %bitcast.46) | data formatting | bytes 3538944 | tf_op jit(solution)/shard_map/all_to_all | solution.py:34
  105.1 4.0 %fusion.19 = bf16[512,384]{1,0:T(8,128)(2,1)S(1)} fusion(bf16[3,384,768]{2,1,0:T(8,128)(2,1)} %param.4, bf16[512,1,768]{2,0,1:T(8,128)(2,1)} %get-tuple-element.5, bf16[512,1,768]{2,0,1:T(8,128)(2,1)} %get-tuple-element.4, bf16[512,1,768]{2,0,1:T(8,128)(2,1)} %get-tuple-element.6, f32[512,384]{1,0:T(8,128)S(1)} %reduce_sum.9, ...), kind=kOutput, calls=%fused_computation.26 | convolution fusion | flops 913047552 | bytes 5701632 | tf_op jit(solution)/shard_map/tko,kio->ti/dot_general | solution.py:45
  109.6 1.2 convert_element_type.60
  110.8 1.9 %pad_maximum_fusion = bf16[512,3,768]{2,0,1:T(8,128)(2,1)S(1)} fusion(bf16[512,1,768]{2,0,1:T(8,128)(2,1)} %get-tuple-element.7, bf16[512,1,768]{2,0,1:T(8,128)(2,1)} %get-tuple-element.8, bf16[512,1,768]{2,0,1:T(8,128)(2,1)} %get-tuple-element.9), kind=kLoop, calls=%fused_computation | loop fusion | flops 2359296 | bytes 4718592 | tf_op jit(solution)/shard_map/stack | solution.py:35
  112.7 2.5 %copy.20 = bf16[512,3,768]{0,2,1:T(8,128)(2,1)} copy(bf16[512,3,768]{2,0,1:T(8,128)(2,1)S(1)} %pad_maximum_fusion) | data formatting | bytes 4718592 | tf_op jit(solution)/shard_map/stack | solution.py:35
  115.2 4.4 %fusion.10 = bf16[1,512,384]{2,1,0:T(8,128)(2,1)} fusion(bf16[512,2304]{0,1:T(8,128)(2,1)} %bitcast.45, bf16[2304,384]{1,0:T(8,128)(2,1)} %bitcast.47, f32[512,384]{1,0:T(8,128)S(1)} %reduce_sum.9), kind=kOutput, calls=%fused_computation.12 | convolution fusion | flops 906559488 | bytes 5308416 | tf_op jit(solution)/shard_map/dot_general | solution.py:36
  119.6 50.3 %all-reduce.2.cloned.1.call-done = f32[3,384,384]{2,1,0:T(8,128)} async-done(((f32[3,384,384]{2,1,0:T(8,128)}), f32[3,384,384]{2,1,0:T(8,128)}) %all-reduce.2.cloned.1.call-update) | async-done | bytes 1769488 | tf_op jit(solution)/shard_map/psum | solution.py:66
  169.8 2.8 %copy.37 = f32[3,384,384]{2,1,0:T(8,128)} copy(f32[3,384,384]{2,1,0:T(8,128)} %all-reduce.2.cloned.1.call-done) | data formatting | bytes 3538944
  (15 shorter events, 2.2 us)
Async XLA Ops:
  7.2 35.7 %all-gather.2.cloned.1.call-start = ((), (), s32[]{:S(2)}) async-start(), calls=%async_computation.1 | async-start | bytes 4718592 | tf_op jit(solution)/shard_map/all_gather | solution.py:32
  9.4 2.2 %copy-start = (bf16[1,512,384]{2,1,0:T(8,128)(2,1)S(1)}, bf16[1,512,384]{2,1,0:T(8,128)(2,1)}, u32[]{:S(2)}) copy-start(bf16[1,512,384]{2,1,0:T(8,128)(2,1)} %param.5) | copy-start | bytes 1179652
  11.7 13.3 %collective-permute-start = (bf16[2,256,384]{2,1,0:T(8,128)(2,1)S(1)}, bf16[2,256,384]{2,1,0:T(8,128)(2,1)S(1)}, u32[]{:S(2)}, u32[]{:S(2)}) collective-permute-start(bf16[2,256,384]{2,1,0:T(8,128)(2,1)S(1)} %get-tuple-element.14), channel_id=1, source_target_pairs={{0,4},{4,8},{8,12},{1,5},{5,9},{9,13},{2,6},{6,10},{10,14},{3,7},{... | collective-permute-start | bytes 1179656 | tf_op jit(solution)/shard_map/ppermute | solution.py:10
  16.7 12.5 %collective-permute-start.1 = (bf16[2,256,384]{2,1,0:T(8,128)(2,1)S(1)}, bf16[2,256,384]{2,1,0:T(8,128)(2,1)S(1)}, u32[]{:S(2)}, u32[]{:S(2)}) collective-permute-start(bf16[2,256,384]{2,1,0:T(8,128)(2,1)S(1)} %get-tuple-element.15), channel_id=1, source_target_pairs={{4,0},{8,4},{12,8},{5,1},{9,5},{13,9},{6,2},{10,6},{14,10},{7,3},{... | collective-permute-start | bytes 1179656 | tf_op jit(solution)/shard_map/ppermute | solution.py:10
  30.5 139.4 %all-reduce.2.cloned.1.call-start = ((), (), s32[]{:S(2)}) async-start(), calls=%async_computation.2 | async-start | bytes 3538944 | tf_op jit(solution)/shard_map/psum | solution.py:66
  47.6 1.6 copy-start.1
  50.1 40.9 %collective-permute-start.2 = (f32[3,384,384]{2,1,0:T(8,128)S(1)}, f32[3,384,384]{2,1,0:T(8,128)S(1)}, u32[]{:S(2)}, u32[]{:S(2)}) collective-permute-start(f32[3,384,384]{2,1,0:T(8,128)S(1)} %fusion.38), channel_id=1, source_target_pairs={{0,2},{2,0},{1,3},{3,1},{4,6},{6,4},{5,7},{7,5},{8,10},{10,8},{9,1... | collective-permute-start | bytes 5308424 | tf_op jit(solution)/shard_map/ppermute | solution.py:62
Sparse Core Ops, SparseCore 0:
  30.6 12.2 all-gather.1
  93.2 76.6 all-reduce.1
where the time goes:
time: 180 us; the launch traced here: 179 us
  waiting for transfers between devices  112 us (62%)
  local copies, waits for them, and re-layouts  21.9 us (12%)
  between operations  14.2 us (8%)
  matrix products  11.3 us (6%)
  starting transfers between devices  8.15 us (5%)
  other arithmetic  6.57 us (4%)
  blocking collectives  5.63 us (3%)
    psum x1, waiting for transfers between devices, shards(): weight_grad = lax.psum(summed, 'seq')  50.3 us
    ppermute x1, waiting for transfers between devices, shards(): summed = keep + lax.ppermute(send, 'batch', [(0, 1), (1, 0)])  39.1 us
    all_gather x1, waiting for transfers between devices, shards(): full_ext = lax.all_gather(own_ext, 'chan', axis=2, tiled=True)  11.2 us
    ppermute x2, waiting for transfers between devices, shift_from(): return lax.ppermute(block, axis, route)  11.2 us
    unnamed x6, local copies, waits for them, and re-layouts  6.76 us
    ppermute x2, starting transfers between devices, shift_from(): return lax.ppermute(block, axis, route)  6.27 us
    all_to_all x1, blocking collectives, shards(): weight_cols = lax.all_to_all(conv_weight, 'chan', 2, 1, tiled=True)  5.63 us
    slice x1, local copies, waits for them, and re-layouts, shards(): cot_full[(2 - k) * spread:(2 - k) * spread + rows]  4.6 us
  transfers between devices with their start and end apart: 5, of which 5 were waited for; matrix products, arithmetic and copies ran while one was open for 12% of the time, Pallas kernels for 0%

commit v1 on v0

--- a/solution.py
+++ b/solution.py
@@ -63,7 +63,11 @@
     else:
         partial = jnp.einsum("tki,to->kio", own_taps, cot_mid, preferred_element_type=jnp.float32)
         summed = lax.psum_scatter(partial, "batch", scatter_dimension=2, tiled=True)
-    weight_grad = lax.psum(summed, "seq")
+    weight_grad = summed
+    for hop in (1, 2):
+        weight_grad = weight_grad + lax.ppermute(
+            weight_grad, "seq", [(dev, dev ^ hop) for dev in range(4)]
+        )
     return (block_out[None], input_grad[None], weight_grad)
 
 

time: 180 us -> 222 us (1.23)
  waiting for transfers between devices: 112 us -> 149 us
  other arithmetic: 6.57 us -> 11.3 us
  starting transfers between devices: 8.15 us -> 12.6 us
  local copies, waits for them, and re-layouts: 21.9 us -> 19 us
    ppermute x0 -> x2, waiting for transfers between devices: none -> 87.4 us  [shards(): lax.ppermute(weight_grad, 'seq', [(dev, dev ^ hop) for dev in range(4)])]
    psum x1 -> x0, waiting for transfers between devices: 50.3 us -> none  [shards(): weight_grad = lax.psum(summed, 'seq')]
    add x0 -> x2, other arithmetic: none -> 4.79 us  [shards(): weight_grad + lax.ppermute(weight_grad, 'seq', [(dev, dev ^ hop) for dev...]
    ppermute x0 -> x2, starting transfers between devices: none -> 4.49 us  [shards(): lax.ppermute(weight_grad, 'seq', [(dev, dev ^ hop) for dev in range(4)])]
    unnamed x6 -> x5, local copies, waits for them, and re-layouts: 6.76 us -> 3.96 us
  transfers between devices with their start and end apart: 5 -> 6, of which waited for: 5 -> 6; matrix products, arithmetic and copies ran while one was open for 12% -> 10% of each run, Pallas kernels for 0% -> 0%
where the time goes in v1:
time: 222 us
  waiting for transfers between devices  149 us (67%)
  local copies, waits for them, and re-layouts  19 us (9%)
  between operations  14.2 us (6%)
  starting transfers between devices  12.6 us (6%)
  other arithmetic  11.3 us (5%)
  matrix products  10 us (5%)
  blocking collectives  5.63 us (3%)
    ppermute x2, waiting for transfers between devices, shards(): lax.ppermute(weight_grad, 'seq', [(dev, dev ^ hop) for dev in range(4)])  87.4 us
    ppermute x1, waiting for transfers between devices, shards(): summed = keep + lax.ppermute(send, 'batch', [(0, 1), (1, 0)])  39.1 us
    all_gather x1, waiting for transfers between devices, shards(): full_ext = lax.all_gather(own_ext, 'chan', axis=2, tiled=True)  11.3 us
    ppermute x2, waiting for transfers between devices, shift_from(): return lax.ppermute(block, axis, route)  11.2 us
    ppermute x2, starting transfers between devices, shift_from(): return lax.ppermute(block, axis, route)  6.27 us
    all_to_all x1, blocking collectives, shards(): weight_cols = lax.all_to_all(conv_weight, 'chan', 2, 1, tiled=True)  5.63 us
    add x2, other arithmetic, shards(): weight_grad + lax.ppermute(weight_grad, 'seq', [(dev, dev ^ hop) for dev...  4.79 us
    slice x1, local copies, waits for them, and re-layouts, shards(): cot_full[(2 - k) * spread:(2 - k) * spread + rows]  4.55 us
  transfers between devices with their start and end apart: 6, of which 6 were waited for; matrix products, arithmetic and copies ran while one was open for 10% of the time, Pallas kernels for 0%

profile of v1, /device:TPU:0, one launch (start us, length us, event | category | flops | bytes accessed | tf_op | source)
XLA Modules:
  0.0 221.7 jit_solution(17003445993316854878)
XLA Ops:
  7.2 2.2 reshape.129
  9.4 1.9 reduce_sum.9
  11.7 5.0 %collective-permute-start = (bf16[2,256,384]{2,1,0:T(8,128)(2,1)S(1)}, bf16[2,256,384]{2,1,0:T(8,128)(2,1)S(1)}, u32[]{:S(2)}, u32[]{:S(2)}) collective-permute-start(bf16[2,256,384]{2,1,0:T(8,128)(2,1)S(1)} %get-tuple-element.14), channel_id=1, source_target_pairs={{0,4},{4,8},{8,12},{1,5},{5,9},{9,13},{2,6},{6,10},{10,14},{3,7},{... | collective-permute-start | bytes 1179656 | tf_op jit(solution)/shard_map/ppermute | solution.py:10
  18.0 7.0 %collective-permute-done = bf16[2,256,384]{2,1,0:T(8,128)(2,1)S(1)} collective-permute-done((bf16[2,256,384]{2,1,0:T(8,128)(2,1)S(1)}, bf16[2,256,384]{2,1,0:T(8,128)(2,1)S(1)}, u32[]{:S(2)}, u32[]{:S(2)}) %collective-permute-start) | collective-permute-done | bytes 393248 | tf_op jit(solution)/shard_map/ppermute | solution.py:10
  25.0 4.1 %collective-permute-done.1 = bf16[2,256,384]{2,1,0:T(8,128)(2,1)S(1)} collective-permute-done((bf16[2,256,384]{2,1,0:T(8,128)(2,1)S(1)}, bf16[2,256,384]{2,1,0:T(8,128)(2,1)S(1)}, u32[]{:S(2)}, u32[]{:S(2)}) %collective-permute-start.1) | collective-permute-done | bytes 393248 | tf_op jit(solution)/shard_map/ppermute | solution.py:10
  29.1 1.3 pad_maximum_fusion.1
  31.6 11.3 %all-gather.2.cloned.1.call-done = bf16[2,1024,768]{2,1,0:T(8,128)(2,1)} async-done(((bf16[2,1024,384]{2,1,0:T(8,128)(2,1)}), bf16[2,1024,768]{2,1,0:T(8,128)(2,1)}) %all-gather.2.cloned.1.call-update) | async-done | bytes 3145744 | tf_op jit(solution)/shard_map/all_gather | solution.py:32
  42.8 4.5 %fusion.45 = (bf16[1,512,768]{2,1,0:T(8,128)(2,1)S(1)}, bf16[512,1,768]{2,0,1:T(8,128)(2,1)}, bf16[512,1,768]{2,0,1:T(8,128)(2,1)}, bf16[512,1,768]{2,0,1:T(8,12...) fusion(bf16[2,1024,768]{2,1,0:T(8,128)(2,1)} %all-gather.2.cloned.1.call-done), kind=kLoop, calls=%fused_computation.67 | loop fusion | bytes 10223616 | tf_op jit(solution)/shard_map/slice | solution.py:43
  47.6 1.6 constant_dynamic-slice_fusion.1
  50.1 1.8 collective-permute-start.2
  51.9 39.1 %collective-permute-done.2 = f32[3,384,384]{2,1,0:T(8,128)S(1)} collective-permute-done((f32[3,384,384]{2,1,0:T(8,128)S(1)}, f32[3,384,384]{2,1,0:T(8,128)S(1)}, u32[]{:S(2)}, u32[]{:S(2)}) %collective-permute-start.2) | collective-permute-done | bytes 1769504 | tf_op jit(solution)/shard_map/ppermute | solution.py:62
  91.8 1.8 collective-permute-start.3
  93.6 38.2 %collective-permute-done.3 = f32[3,384,384]{2,1,0:T(8,128)S(1)} collective-permute-done((f32[3,384,384]{2,1,0:T(8,128)S(1)}, f32[3,384,384]{2,1,0:T(8,128)S(1)}, u32[]{:S(2)}, u32[]{:S(2)}) %collective-permute-start.3) | collective-permute-done | bytes 1769504 | tf_op jit(solution)/shard_map/ppermute | solution.py:68
  131.8 1.4 add.79
  133.2 2.7 %collective-permute-start.4 = (f32[3,384,384]{2,1,0:T(8,128)}, f32[3,384,384]{2,1,0:T(8,128)}, u32[]{:S(2)}, u32[]{:S(2)}) collective-permute-start(f32[3,384,384]{2,1,0:T(8,128)} %add.79), channel_id=1, source_target_pairs={{0,8},{4,12},{8,0},{12,4},{1,9},{5,13},{9,1},{13,5},{2,10},{6,14},... | collective-permute-start | bytes 5308424 | tf_op jit(solution)/shard_map/ppermute | solution.py:68
  135.9 4.0 %copy.21 = bf16[3,384,768]{1,0,2:T(4,128)(2,1)S(1)} copy(bf16[3,384,768]{2,1,0:T(8,128)(2,1)} %param.4) | data formatting | bytes 3538944 | tf_op args[1]
  139.8 5.6 %all_to_all.15 = bf16[3,384,768]{1,0,2:T(4,128)(2,1)S(1)} all-to-all(bf16[3,384,768]{1,0,2:T(4,128)(2,1)S(1)} %copy.21), channel_id=1, replica_groups=mesh['group'=2,'seq'=4,'batch'=2,'chan'=2] {'chan'}, dimensions={2} | all-to-all | bytes 3538944 | tf_op jit(solution)/shard_map/all_to_all | solution.py:34
  145.7 2.3 %copy.23 = bf16[3,2,384,384]{3,2,1,0:T(8,128)(2,1)} copy(bf16[3,2,384,384]{2,3,1,0:T(8,128)(2,1)S(1)} %bitcast.46) | data formatting | bytes 3538944 | tf_op jit(solution)/shard_map/all_to_all | solution.py:34
  148.0 4.0 %fusion.19 = bf16[512,384]{1,0:T(8,128)(2,1)S(1)} fusion(bf16[3,384,768]{2,1,0:T(8,128)(2,1)} %param.4, bf16[512,1,768]{2,0,1:T(8,128)(2,1)} %get-tuple-element.5, bf16[512,1,768]{2,0,1:T(8,128)(2,1)} %get-tuple-element.4, bf16[512,1,768]{2,0,1:T(8,128)(2,1)} %get-tuple-element.6, f32[512,384]{1,0:T(8,128)S(1)} %reduce_sum.9, ...), kind=kOutput, calls=%fused_computation.26 | convolution fusion | flops 913047552 | bytes 5701632 | tf_op jit(solution)/shard_map/tko,kio->ti/dot_general | solution.py:45
  153.6 1.9 pad_maximum_fusion
  155.4 2.5 %copy.20 = bf16[512,3,768]{0,2,1:T(8,128)(2,1)} copy(bf16[512,3,768]{2,0,1:T(8,128)(2,1)S(1)} %pad_maximum_fusion) | data formatting | bytes 4718592 | tf_op jit(solution)/shard_map/stack | solution.py:35
  157.9 4.4 %fusion.10 = bf16[1,512,384]{2,1,0:T(8,128)(2,1)} fusion(bf16[512,2304]{0,1:T(8,128)(2,1)} %bitcast.45, bf16[2304,384]{1,0:T(8,128)(2,1)} %bitcast.47, f32[512,384]{1,0:T(8,128)S(1)} %reduce_sum.9), kind=kOutput, calls=%fused_computation.12 | convolution fusion | flops 906559488 | bytes 5308416 | tf_op jit(solution)/shard_map/dot_general | solution.py:36
  162.3 49.2 %collective-permute-done.4 = f32[3,384,384]{2,1,0:T(8,128)} collective-permute-done((f32[3,384,384]{2,1,0:T(8,128)}, f32[3,384,384]{2,1,0:T(8,128)}, u32[]{:S(2)}, u32[]{:S(2)}) %collective-permute-start.4) | collective-permute-done | bytes 1769504 | tf_op jit(solution)/shard_map/ppermute | solution.py:68
  211.5 3.4 %add.80 = f32[3,384,384]{2,1,0:T(8,128)} add(f32[3,384,384]{2,1,0:T(8,128)} %add.79, f32[3,384,384]{2,1,0:T(8,128)} %collective-permute-done.4) | non-fusion elementwise | flops 442368 | bytes 5308416 | tf_op jit(solution)/shard_map/add | solution.py:68
  (17 shorter events, 6.5 us)
Async XLA Ops:
  7.2 35.7 %all-gather.2.cloned.1.call-start = ((), (), s32[]{:S(2)}) async-start(), calls=%async_computation.1 | async-start | bytes 4718592 | tf_op jit(solution)/shard_map/all_gather | solution.py:32
  9.4 2.2 copy-start
  11.7 13.3 %collective-permute-start = (bf16[2,256,384]{2,1,0:T(8,128)(2,1)S(1)}, bf16[2,256,384]{2,1,0:T(8,128)(2,1)S(1)}, u32[]{:S(2)}, u32[]{:S(2)}) collective-permute-start(bf16[2,256,384]{2,1,0:T(8,128)(2,1)S(1)} %get-tuple-element.14), channel_id=1, source_target_pairs={{0,4},{4,8},{8,12},{1,5},{5,9},{9,13},{2,6},{6,10},{10,14},{3,7},{... | collective-permute-start | bytes 1179656 | tf_op jit(solution)/shard_map/ppermute | solution.py:10
  16.7 12.5 %collective-permute-start.1 = (bf16[2,256,384]{2,1,0:T(8,128)(2,1)S(1)}, bf16[2,256,384]{2,1,0:T(8,128)(2,1)S(1)}, u32[]{:S(2)}, u32[]{:S(2)}) collective-permute-start(bf16[2,256,384]{2,1,0:T(8,128)(2,1)S(1)} %get-tuple-element.15), channel_id=1, source_target_pairs={{4,0},{8,4},{12,8},{5,1},{9,5},{13,9},{6,2},{10,6},{14,10},{7,3},{... | collective-permute-start | bytes 1179656 | tf_op jit(solution)/shard_map/ppermute | solution.py:10
  47.6 1.6 copy-start.1
  50.1 40.9 %collective-permute-start.2 = (f32[3,384,384]{2,1,0:T(8,128)S(1)}, f32[3,384,384]{2,1,0:T(8,128)S(1)}, u32[]{:S(2)}, u32[]{:S(2)}) collective-permute-start(f32[3,384,384]{2,1,0:T(8,128)S(1)} %fusion.38), channel_id=1, source_target_pairs={{0,2},{2,0},{1,3},{3,1},{4,6},{6,4},{5,7},{7,5},{8,10},{10,8},{9,1... | collective-permute-start | bytes 5308424 | tf_op jit(solution)/shard_map/ppermute | solution.py:62
  91.8 40.0 %collective-permute-start.3 = (f32[3,384,384]{2,1,0:T(8,128)S(1)}, f32[3,384,384]{2,1,0:T(8,128)S(1)}, u32[]{:S(2)}, u32[]{:S(2)}) collective-permute-start(f32[3,384,384]{2,1,0:T(8,128)S(1)} %convolution_add_fusion), channel_id=1, source_target_pairs={{0,4},{4,0},{8,12},{12,8},{1,5},{5,1},{9,13},{13,9},{2,6},{6,2},{1... | collective-permute-start | bytes 5308424 | tf_op jit(solution)/shard_map/ppermute | solution.py:68
  133.2 78.3 %collective-permute-start.4 = (f32[3,384,384]{2,1,0:T(8,128)}, f32[3,384,384]{2,1,0:T(8,128)}, u32[]{:S(2)}, u32[]{:S(2)}) collective-permute-start(f32[3,384,384]{2,1,0:T(8,128)} %add.79), channel_id=1, source_target_pairs={{0,8},{4,12},{8,0},{12,4},{1,9},{5,13},{9,1},{13,5},{2,10},{6,14},... | collective-permute-start | bytes 5308424 | tf_op jit(solution)/shard_map/ppermute | solution.py:68
Sparse Core Ops, SparseCore 0:
  30.6 12.2 all-gather.1
